TPU v7x, 256 devices: a whole 4x4x8 slice. The times are simulated.
256 devices in a mesh: seq: 64 (over y, x_lo, z), dp: 4 (over x_hi, core).
Axes of the slice: x: 4 (x_hi: 2, x_lo: 2; x = x_hi * 2 + x_lo), y: 4, z: 8, core: 2. Of those that a mesh axis runs over, the one named last changes fastest.
Arguments:
- inputs: float32 [4, 32768, 256], P('dp', 'seq'), may hold values from -6 to 6
- out_cotangent: float32 [4, 32768, 256], P('dp', 'seq'), may hold values from -6 to 6
- skip_cotangent: float32 [4, 32768, 256], P('dp', 'seq'), may hold values from -6 to 6
- convolution_weight: float32 [2, 512, 1024], replicated, may hold values from -0.25 to 0.25
- convolution_bias: float32 [2, 1024], replicated, may hold values from -3 to 3
- output_weight: float32 [2, 512, 512], replicated, may hold values from -0.25 to 0.25
Outputs:
- input_grad: float32 [4, 32768, 256], P('dp', 'seq')
- conv_grad: float32 [1024, 1024], P(('seq', 'dp'))
- out_grad: float32 [1024, 512], P(('seq', 'dp'))
- bias_grad: float32 [2048], P(('seq', 'dp'))
All inputs are finite; a program needn't handle non-finite values.
Results may differ from a plain program's by a relative error of at most 0.00025.
Values sent between devices are 32-bit elements; how exact they have to be, the bound alone decides.
No kernel may reach another device: no remote copies, remote signals or barrier semaphores. Data moves between devices by JAX's collectives and lax.ppermute only.
A program may use at most 128 MiB of HBM per device.

v0:
```python
import math

import jax
import jax.numpy as jnp
from jax import lax
from jax.sharding import PartitionSpec as P


def from_behind(block, axis, distance):
    devices = range(lax.axis_size(axis))
    route = [(i - distance, i) for i in devices if i - distance in devices]
    return lax.ppermute(block, axis, route)


def matmul(left, right):
    return jnp.dot(left, right, precision=lax.Precision.HIGHEST, preferred_element_type=jnp.float32)


def contract(left, right, left_dim, right_dim):
    return lax.dot_general(
        left,
        right,
        (((left_dim,), (right_dim,)), ((), ())),
        precision=lax.Precision.HIGHEST,
        preferred_element_type=jnp.float32,
    )


def layer_forward_step(earlier, values, weight, bias):
    joined = jnp.concatenate([earlier, values], axis=1)
    mixed = matmul(joined, weight) + bias
    width = weight.shape[1] // 2
    tanh_part = jnp.tanh(mixed[:, :width])
    sigm_part = jax.nn.sigmoid(mixed[:, width:])
    return (joined, tanh_part, sigm_part, tanh_part * sigm_part)


def layer_backward_step(
    joined, tanh_part, sigm_part, hidden, weight, out_w, carried_state, skip_cotangent_rows
):
    channels = carried_state.shape[1]
    outer = jnp.concatenate([carried_state, skip_cotangent_rows], axis=1)
    dhidden = contract(outer, out_w, 1, 1)
    dfilter = dhidden * sigm_part * (1.0 - tanh_part * tanh_part)
    dgate = dhidden * tanh_part * sigm_part * (1.0 - sigm_part)
    dmixed = jnp.concatenate([dfilter, dgate], axis=1)
    out_t = contract(outer, hidden, 0, 0)
    conv_g = contract(joined, dmixed, 0, 0)
    bias_g = jnp.sum(dmixed, axis=0)
    back = contract(dmixed, weight, 1, 1)
    return (back[:, :channels], back[:, channels:], conv_g, out_t, bias_g)


def local(
    inputs, out_cotangent, skip_cotangent, convolution_weight, convolution_bias, output_weight
):
    start_row = inputs[0]
    output_cotangent_rows = out_cotangent[0]
    skip_cotangent_rows = skip_cotangent[0]
    rows, channels = start_row.shape
    half = rows // 2
    tail = from_behind(start_row[rows - half :], "seq", 1)
    earlier1 = jnp.concatenate([tail, start_row[: rows - half]], axis=0)
    first_joined, first_tanh, first_sigmoid, first_hidden = layer_forward_step(
        earlier1, start_row, convolution_weight[0], convolution_bias[0]
    )
    second_layer = start_row + matmul(first_hidden, output_weight[0][:, :channels])
    earlier2 = from_behind(second_layer, "seq", 1)
    second_joined, second_tanh, second_sigmoid, second_hidden = layer_forward_step(
        earlier2, second_layer, convolution_weight[1], convolution_bias[1]
    )
    past2, local2, second_conv_output, second_output, second_bias = layer_backward_step(
        second_joined,
        second_tanh,
        second_sigmoid,
        second_hidden,
        convolution_weight[1],
        output_weight[1],
        output_cotangent_rows,
        skip_cotangent_rows,
    )
    carried_state = output_cotangent_rows + local2 + from_behind(past2, "seq", -1)
    past1, local1, first_conv_output, first_output, first_bias = layer_backward_step(
        first_joined,
        first_tanh,
        first_sigmoid,
        first_hidden,
        convolution_weight[0],
        output_weight[0],
        carried_state,
        skip_cotangent_rows,
    )
    rim_rows = from_behind(past1[:half], "seq", -1)
    input_grad = carried_state + local1 + jnp.concatenate([past1[half:], rim_rows], axis=0)
    factor = 1.0 / math.sqrt(rows * lax.axis_size("seq") * lax.axis_size("dp"))
    conv_terms = jnp.concatenate([first_conv_output, second_conv_output], axis=0) * factor
    out_terms = jnp.concatenate([first_output, second_output], axis=0) * factor
    bias_terms = jnp.concatenate([first_bias, second_bias], axis=0) * factor
    conv_grad, out_grad, bias_grad = (
        lax.psum_scatter(conv_terms, ("seq", "dp"), scatter_dimension=0, tiled=True),
        lax.psum_scatter(out_terms, ("seq", "dp"), scatter_dimension=0, tiled=True),
        lax.psum_scatter(bias_terms, ("seq", "dp"), scatter_dimension=0, tiled=True),
    )
    return (input_grad[None], conv_grad, out_grad, bias_grad)


def solution(mesh):
    return jax.shard_map(
        local,
        mesh=mesh,
        in_specs=(P("dp", "seq", None), P("dp", "seq", None), P("dp", "seq", None), P(), P(), P()),
        out_specs=(
            P("dp", "seq", None),
            P(("seq", "dp"), None),
            P(("seq", "dp"), None),
            P(("seq", "dp")),
        ),
        check_vma=False,
    )
```

profile of v0, /device:TPU:10, one launch (start us, length us, event | category | flops | bytes accessed | tf_op | source)
XLA Modules:
  0.0 369.1 jit_solution(9473015300284220920)
XLA Ops:
  7.2 0.0 copy-start.16
  7.2 0.0 all-reduce.6.cloned.1.call-start
  7.2 1.2 copy.23
  8.5 0.0 copy-start.3
  8.5 3.8 %collective-permute-start = (f32[256,256]{0,1:T(8,128)S(1)}, f32[256,256]{0,1:T(8,128)S(1)}, u32[]{:S(2)}, u32[]{:S(2)}) collective-permute-start(f32[256,256]{0,1:T(8,128)S(1)} %get-tuple-element.20), channel_id=1, source_target_pairs={{0,4},{4,8},{8,12},{12,16},{16,20},{20,24},{24,28},{28,32},{32,36}... | collective-permute-start | bytes 786440 | tf_op jit(solution)/shard_map/ppermute | solution.py:12
  12.4 0.0 copy-done.16
  12.4 1.3 slice_bitcast_fusion
  13.7 8.9 %collective-permute-done = f32[256,256]{0,1:T(8,128)S(1)} collective-permute-done((f32[256,256]{0,1:T(8,128)S(1)}, f32[256,256]{0,1:T(8,128)S(1)}, u32[]{:S(2)}, u32[]{:S(2)}) %collective-permute-start) | collective-permute-done | bytes 262176 | tf_op jit(solution)/shard_map/ppermute | solution.py:12
  22.6 5.3 %fusion.12 = f32[512,1024]{0,1:T(8,128)S(1)} fusion(f32[2,512,1024]{2,1,0:T(8,128)} %param.9, f32[1024]{0:T(1024)S(1)} %bitcast.46, f32[512,256]{0,1:T(8,128)S(1)} %bitcast.37, f32[256,256]{0,1:T(8,128)S(1)} %get-tuple-element.21, f32[256,256]{0,1:T(8,128)S(1)} %collective-permute-done), kind=kOutput, calls=%fused_computation.16 | convolution fusion | flops 3222274048 | bytes 5246976 | tf_op jit(solution)/shard_map/dot_general | solution.py:16
  27.8 0.0 copy-done.3
  27.9 0.0 copy-done.12
  27.9 0.0 copy-start.7
  27.9 1.4 convolution_add_fusion
  29.3 0.0 copy-done.7
  29.3 2.1 collective-permute-start.1
  31.4 2.0 copy.21
  33.4 2.0 copy.22
  35.5 10.9 %collective-permute-done.1 = f32[512,256]{0,1:T(8,128)S(1)} collective-permute-done((f32[512,256]{0,1:T(8,128)S(1)}, f32[512,256]{0,1:T(8,128)S(1)}, u32[]{:S(2)}, u32[]{:S(2)}) %collective-permute-start.1) | collective-permute-done | bytes 524320 | tf_op jit(solution)/shard_map/ppermute | solution.py:12
  46.4 5.3 %fusion.15 = f32[512,1024]{0,1:T(8,128)S(1)} fusion(f32[2,512,1024]{2,1,0:T(8,128)} %param.9, f32[1024]{0:T(1024)S(1)} %bitcast.45, f32[512,256]{0,1:T(8,128)S(1)} %convolution_add_fusion, f32[512,256]{0,1:T(8,128)S(1)} %collective-permute-done.1), kind=kOutput, calls=%fused_computation.17 | convolution fusion | flops 3222011904 | bytes 5246976 | tf_op jit(solution)/shard_map/dot_general | solution.py:16
  51.7 0.0 copy-done.9
  51.7 0.0 copy-done.14
  51.7 0.0 copy-done.15
  51.8 0.0 copy-start
  51.8 2.3 subtract_multiply_fusion.3
  54.0 0.0 copy-done
  54.1 3.6 fusion
  57.7 2.1 collective-permute-start.2
  59.9 3.6 fusion.21
  63.5 2.1 fusion.30
  65.5 0.0 copy-start.8
  65.6 6.2 %collective-permute-done.2 = f32[512,256]{0,1:T(8,128)S(1)} collective-permute-done((f32[512,256]{0,1:T(8,128)S(1)}, f32[512,256]{0,1:T(8,128)S(1)}, u32[]{:S(2)}, u32[]{:S(2)}) %collective-permute-start.2) | collective-permute-done | bytes 524320 | tf_op jit(solution)/shard_map/ppermute | solution.py:12
  71.8 0.1 fusion.38
  71.9 0.0 copy-done.8
  72.0 0.0 copy-start.10
  72.0 2.1 fusion.33
  74.1 0.0 copy-done.10
  74.1 2.3 subtract_multiply_fusion.1
  76.4 0.0 copy-start.1
  76.4 0.0 copy-start.4
  76.4 0.0 copy-start.13
  76.4 1.6 maximum_multiply_fusion.1
  78.0 0.0 copy-done.1
  78.1 0.0 copy-done.4
  78.1 0.0 copy-done.13
  78.1 3.9 %fusion.19 = f32[512,1024]{1,0:T(8,128)S(1)} fusion(f32[512,512]{0,1:T(8,128)S(1)} %get-tuple-element.15, f32[512,512]{0,1:T(8,128)S(1)} %get-tuple-element.14, f32[512,256]{0,1:T(8,128)S(1)} %bitcast.38, f32[256,256]{0,1:T(8,128)S(1)} %get-tuple-element.21, f32[256,256]{0,1:T(8,128)S(1)} %copy-done.13), kind=kOutput, calls=%fused_computation.19 | convolution fusion | flops 3222274048 | bytes 5242880 | tf_op jit(solution)/shard_map/dot_general | solution.py:20
  82.0 2.5 maximum_multiply_fusion
  84.5 0.0 all-reduce.6.cloned.1.call-update
  84.5 5.4 %fusion.4 = f32[512,512]{0,1:T(8,128)S(1)} fusion(f32[2,512,1024]{2,1,0:T(8,128)} %param.9, f32[512,512]{0,1:T(8,128)} %copy-done.1, f32[512,512]{0,1:T(8,128)S(1)} %get-tuple-element.14), kind=kOutput, calls=%fused_computation.8 | convolution fusion | flops 3221749760 | bytes 5242880 | tf_op jit(solution)/shard_map/dot_general | solution.py:20
  90.0 0.0 copy-start.5
  90.0 1.0 copy-done.5
  90.9 0.7 fusion.55
  91.7 4.3 %collective-permute-start.3 = (f32[256,256]{0,1:T(8,128)}, f32[256,256]{0,1:T(8,128)}, u32[]{:S(2)}, u32[]{:S(2)}) collective-permute-start(f32[256,256]{0,1:T(8,128)} %get-tuple-element.19), channel_id=1, source_target_pairs={{4,0},{8,4},{12,8},{16,12},{20,16},{24,20},{28,24},{32,28},{36,32}... | collective-permute-start | bytes 786440 | tf_op jit(solution)/shard_map/ppermute | solution.py:12
  96.0 0.0 copy-start.2
  96.0 0.2 fusion.20
  96.2 1.0 copy-done.2
  97.2 0.2 fusion.18
  97.5 74.4 %all-reduce.2 = f32[2048]{0:T(1024)S(1)} all-reduce(f32[2048]{0:T(1024)S(1)} %maximum_multiply_fusion.2), channel_id=4, replica_groups=mesh['seq'=64,'dp'=4] {'seq','dp'}, use_global_device_ids=true, to_apply=%region_4.0.clone | all-reduce | flops 2048 | bytes 16384
  171.8 0.6 dynamic-slice.2
  172.4 0.0 collective-permute-done.3
  172.4 1.1 fusion.37
  173.5 1.0 copy.31
  174.5 185.0 %all-reduce.6.cloned.1.call-done = (f32[1024,1024]{1,0:T(8,128)}, f32[1024,512]{1,0:T(8,128)}) async-done(((f32[1024,1024]{1,0:T(8,128)}, f32[1024,512]{1,0:T(8,128)}), (f32[1024,1024]{1,0:T(8,128)}, f32[1024,512]{1,0:T(8,128)})) %all-reduce.6.cloned.1.call-update) | async-done | bytes 6291472
  359.5 1.4 constant_dynamic-slice_fusion.1
  360.9 1.3 constant_dynamic-slice_fusion
  (12 shorter events, 0.1 us)
Async XLA Ops:
  7.2 5.2 %copy-start.16 = (f32[2,1024]{1,0:T(2,128)S(1)}, f32[2,1024]{1,0:T(2,128)}, u32[]{:S(2)}) copy-start(f32[2,1024]{1,0:T(2,128)} %param.10) | copy-start | bytes 24580
  7.2 352.4 %all-reduce.6.cloned.1.call-start = ((), (), s32[]{:S(2)}) async-start(), calls=%async_computation | async-start | bytes 12582912
  8.5 19.4 %copy-start.3 = (f32[1,512,256]{1,2,0:T(8,128)}, f32[1,512,256]{1,2,0:T(8,128)S(1)}, u32[]{:S(2)}) copy-start(f32[1,512,256]{1,2,0:T(8,128)S(1)} %copy.23) | copy-start | bytes 1572868
  8.5 14.0 %collective-permute-start = (f32[256,256]{0,1:T(8,128)S(1)}, f32[256,256]{0,1:T(8,128)S(1)}, u32[]{:S(2)}, u32[]{:S(2)}) collective-permute-start(f32[256,256]{0,1:T(8,128)S(1)} %get-tuple-element.20), channel_id=1, source_target_pairs={{0,4},{4,8},{8,12},{12,16},{16,20},{20,24},{24,28},{28,32},{32,36}... | collective-permute-start | bytes 786440 | tf_op jit(solution)/shard_map/ppermute | solution.py:12
  22.6 5.3 %copy-start.12 = (f32[256,256]{0,1:T(8,128)}, f32[256,256]{0,1:T(8,128)S(1)}, u32[]{:S(2)}) copy-start(f32[256,256]{0,1:T(8,128)S(1)} %collective-permute-done) | copy-start | bytes 786436
  27.9 1.4 copy-start.7
  29.3 17.1 %collective-permute-start.1 = (f32[512,256]{0,1:T(8,128)S(1)}, f32[512,256]{0,1:T(8,128)S(1)}, u32[]{:S(2)}, u32[]{:S(2)}) collective-permute-start(f32[512,256]{0,1:T(8,128)S(1)} %convolution_add_fusion), channel_id=1, source_target_pairs={{0,4},{4,8},{8,12},{12,16},{16,20},{20,24},{24,28},{28,32},{32,36}... | collective-permute-start | bytes 1572872 | tf_op jit(solution)/shard_map/ppermute | solution.py:12
  46.4 5.3 %copy-start.9 = (f32[1,512,256]{1,2,0:T(8,128)S(1)}, f32[1,512,256]{1,2,0:T(8,128)}, u32[]{:S(2)}) copy-start(f32[1,512,256]{1,2,0:T(8,128)} %copy.21) | copy-start | bytes 1572868
  46.4 5.4 %copy-start.14 = (f32[2,512,512]{2,1,0:T(8,128)S(1)}, f32[2,512,512]{2,1,0:T(8,128)}, u32[]{:S(2)}) copy-start(f32[2,512,512]{2,1,0:T(8,128)} %param.11) | copy-start | bytes 6291460
  46.4 5.4 %copy-start.15 = (f32[1,512,256]{1,2,0:T(8,128)S(1)}, f32[1,512,256]{1,2,0:T(8,128)}, u32[]{:S(2)}) copy-start(f32[1,512,256]{1,2,0:T(8,128)} %copy.22) | copy-start | bytes 1572868
  51.8 2.3 copy-start
  57.7 14.1 %collective-permute-start.2 = (f32[512,256]{0,1:T(8,128)S(1)}, f32[512,256]{0,1:T(8,128)S(1)}, u32[]{:S(2)}, u32[]{:S(2)}) collective-permute-start(f32[512,256]{0,1:T(8,128)S(1)} %slice.94), channel_id=1, source_target_pairs={{4,0},{8,4},{12,8},{16,12},{20,16},{24,20},{28,24},{32,28},{36,32}... | collective-permute-start | bytes 1572872 | tf_op jit(solution)/shard_map/ppermute | solution.py:12
  65.5 6.4 %copy-start.8 = (f32[512,1024]{0,1:T(8,128)S(1)}, f32[512,1024]{0,1:T(8,128)}, u32[]{:S(2)}) copy-start(f32[512,1024]{0,1:T(8,128)} %copy-done.7) | copy-start | bytes 6291460
  72.0 2.1 copy-start.10
  76.4 1.7 copy-start.1
  76.4 1.7 copy-start.4
  76.4 1.7 copy-start.13
  90.0 1.0 copy-start.5
  91.7 80.7 %collective-permute-start.3 = (f32[256,256]{0,1:T(8,128)}, f32[256,256]{0,1:T(8,128)}, u32[]{:S(2)}, u32[]{:S(2)}) collective-permute-start(f32[256,256]{0,1:T(8,128)} %get-tuple-element.19), channel_id=1, source_target_pairs={{4,0},{8,4},{12,8},{16,12},{20,16},{24,20},{28,24},{32,28},{36,32}... | collective-permute-start | bytes 786440 | tf_op jit(solution)/shard_map/ppermute | solution.py:12
  96.0 1.2 copy-start.2
  97.2 75.2 %copy-start.6 = (f32[512,512]{0,1:T(8,128)S(1)}, f32[512,512]{0,1:T(8,128)}, u32[]{:S(2)}) copy-start(f32[512,512]{0,1:T(8,128)} %copy-done.5) | copy-start | bytes 3145732
  97.2 75.2 %copy-start.11 = (f32[512,256]{0,1:T(8,128)S(1)}, f32[512,256]{0,1:T(8,128)}, u32[]{:S(2)}) copy-start(f32[512,256]{0,1:T(8,128)} %copy-done.10) | copy-start | bytes 1572868
Sparse Core Ops, SparseCore 0:
  84.6 274.8 all-reduce.5
where the time goes:
time: 370 us; the launch traced here: 369 us
  waiting for transfers between devices  211 us (57%)
  blocking collectives  74.4 us (20%)
  matrix products  37.2 us (10%)
  between operations  14.4 us (4%)
  local copies, waits for them, and re-layouts  13.8 us (4%)
  starting transfers between devices  12.4 us (3%)
  other arithmetic  5.84 us (2%)
    unnamed x2, waiting for transfers between devices  185 us
    unnamed x1, blocking collectives  74.4 us
    ppermute x4, waiting for transfers between devices, from_behind(): return lax.ppermute(block, axis, route)  26 us
    dot_general x8, matrix products, contract(): lax.dot_general(left, right, (((left_dim,), (right_dim,)), ((), ())), pre...  25.2 us
    ppermute x4, starting transfers between devices, from_behind(): return lax.ppermute(block, axis, route)  12.4 us
    dot_general x3, matrix products, matmul(): jnp.dot(left, right, precision=lax.Precision.HIGHEST, preferred_element_t...  12 us
    unnamed x41, local copies, waits for them, and re-layouts  11.6 us
  transfers between devices with their start and end apart: 5, of which 4 were waited for; matrix products, arithmetic and copies ran while one was open for 6% of the time, Pallas kernels for 0%

commit v1 on v0

--- a/solution.py
+++ b/solution.py
@@ -4,6 +4,9 @@
 import jax.numpy as jnp
 from jax import lax
 from jax.sharding import PartitionSpec as P
+
+
+SEQ_AXES = ("y", "xl", "z")
 
 
 def from_behind(block, axis, distance):
@@ -59,13 +62,13 @@
     skip_cotangent_rows = skip_cotangent[0]
     rows, channels = start_row.shape
     half = rows // 2
-    tail = from_behind(start_row[rows - half :], "seq", 1)
+    tail = from_behind(start_row[rows - half :], SEQ_AXES, 1)
     earlier1 = jnp.concatenate([tail, start_row[: rows - half]], axis=0)
     first_joined, first_tanh, first_sigmoid, first_hidden = layer_forward_step(
         earlier1, start_row, convolution_weight[0], convolution_bias[0]
     )
     second_layer = start_row + matmul(first_hidden, output_weight[0][:, :channels])
-    earlier2 = from_behind(second_layer, "seq", 1)
+    earlier2 = from_behind(second_layer, SEQ_AXES, 1)
     second_joined, second_tanh, second_sigmoid, second_hidden = layer_forward_step(
         earlier2, second_layer, convolution_weight[1], convolution_bias[1]
     )
@@ -79,7 +82,7 @@
         output_cotangent_rows,
         skip_cotangent_rows,
     )
-    carried_state = output_cotangent_rows + local2 + from_behind(past2, "seq", -1)
+    carried_state = output_cotangent_rows + local2 + from_behind(past2, SEQ_AXES, -1)
     past1, local1, first_conv_output, first_output, first_bias = layer_backward_step(
         first_joined,
         first_tanh,
@@ -90,30 +93,41 @@
         carried_state,
         skip_cotangent_rows,
     )
-    rim_rows = from_behind(past1[:half], "seq", -1)
+    rim_rows = from_behind(past1[:half], SEQ_AXES, -1)
     input_grad = carried_state + local1 + jnp.concatenate([past1[half:], rim_rows], axis=0)
-    factor = 1.0 / math.sqrt(rows * lax.axis_size("seq") * lax.axis_size("dp"))
-    conv_terms = jnp.concatenate([first_conv_output, second_conv_output], axis=0) * factor
-    out_terms = jnp.concatenate([first_output, second_output], axis=0) * factor
+    seq_axes, dp_axes = SEQ_AXES, ("xh", "c")
+    devices = lax.axis_size(seq_axes) * lax.axis_size(dp_axes)
+    factor = 1.0 / math.sqrt(rows * devices)
+    conv_terms = jnp.concatenate([first_conv_output, second_conv_output], axis=0)
+    out_terms = jnp.concatenate([first_output, second_output], axis=0)
     bias_terms = jnp.concatenate([first_bias, second_bias], axis=0) * factor
-    conv_grad, out_grad, bias_grad = (
-        lax.psum_scatter(conv_terms, ("seq", "dp"), scatter_dimension=0, tiled=True),
-        lax.psum_scatter(out_terms, ("seq", "dp"), scatter_dimension=0, tiled=True),
-        lax.psum_scatter(bias_terms, ("seq", "dp"), scatter_dimension=0, tiled=True),
+    conv_rows, out_rows = conv_terms.shape[0] // devices, out_terms.shape[0] // devices
+    packed = jnp.concatenate(
+        [conv_terms.reshape(devices, -1), out_terms.reshape(devices, -1)], axis=1
     )
+    width = packed.shape[1]
+    sizes = [lax.axis_size(a) for a in seq_axes + dp_axes]
+    packed = packed.reshape(*sizes, width).transpose(4, 2, 0, 3, 1, 5)
+    packed = packed.reshape(devices * 8, width // 8)
+    summed = lax.psum_scatter(packed, RING_ORDER, scatter_dimension=0, tiled=True).reshape(-1) * factor
+    split = conv_rows * conv_terms.shape[1]
+    conv_grad = summed[:split].reshape(conv_rows, -1)
+    out_grad = summed[split:].reshape(out_rows, -1)
+    bias_grad = lax.psum_scatter(bias_terms, seq_axes + dp_axes, scatter_dimension=0, tiled=True)
     return (input_grad[None], conv_grad, out_grad, bias_grad)
 
 
+RING_ORDER = ("c", "z", "y", "xh", "xl")
+
+
 def solution(mesh):
+    fine = jax.sharding.Mesh(mesh.devices.reshape(4, 2, 8, 2, 2), ("y", "xl", "z", "xh", "c"))
+    rows_spec = P(("xh", "c"), ("y", "xl", "z"), None)
+    owner = ("y", "xl", "z", "xh", "c")
     return jax.shard_map(
         local,
-        mesh=mesh,
-        in_specs=(P("dp", "seq", None), P("dp", "seq", None), P("dp", "seq", None), P(), P(), P()),
-        out_specs=(
-            P("dp", "seq", None),
-            P(("seq", "dp"), None),
-            P(("seq", "dp"), None),
-            P(("seq", "dp")),
-        ),
+        mesh=fine,
+        in_specs=(rows_spec, rows_spec, rows_spec, P(), P(), P()),
+        out_specs=(rows_spec, P(owner, None), P(owner, None), P(owner)),
         check_vma=False,
     )

time: 370 us -> 542 us (1.46)
  waiting for transfers between devices: 211 us -> 333 us
  local copies, waits for them, and re-layouts: 13.8 us -> 45.6 us
  other arithmetic: 5.84 us -> 17.1 us
    reduce_scatter x0 -> x1, waiting for transfers between devices: none -> 308 us  [local(): lax.psum_scatter(packed, RING_ORDER, scatter_dimension=0, tiled=True)]
    unnamed x2 -> x1, waiting for transfers between devices: 185 us -> 0.02 us
    concatenate x0 -> x4, local copies, waits for them, and re-layouts: none -> 24.3 us  [local(): jnp.concatenate([conv_terms.reshape(devices, -1), out_terms.reshape(devic...]
    transpose x0 -> x1, other arithmetic: none -> 10.7 us  [local(): packed = packed.reshape(*sizes, width).transpose(4, 2, 0, 3, 1, 5)]
    reshape x0 -> x1, local copies, waits for them, and re-layouts: none -> 9.01 us  [local(): packed = packed.reshape(devices * 8, width // 8)]
  transfers between devices with their start and end apart: 5 -> 5, of which waited for: 4 -> 4; matrix products, arithmetic and copies ran while one was open for 6% -> 4% of each run, Pallas kernels for 0% -> 0%
where the time goes in v1:
time: 542 us; the launch traced here: 536 us
  waiting for transfers between devices  333 us (61%)
  blocking collectives  74.2 us (14%)
  local copies, waits for them, and re-layouts  45.6 us (8%)
  matrix products  39.3 us (7%)
  other arithmetic  17.1 us (3%)
  between operations  14.6 us (3%)
  starting transfers between devices  12.5 us (2%)
    reduce_scatter x1, waiting for transfers between devices, local(): lax.psum_scatter(packed, RING_ORDER, scatter_dimension=0, tiled=True)  308 us
    unnamed x1, blocking collectives  74.2 us
    dot_general x8, matrix products, contract(): lax.dot_general(left, right, (((left_dim,), (right_dim,)), ((), ())), pre...  27.3 us
    ppermute x4, waiting for transfers between devices, from_behind(): return lax.ppermute(block, axis, route)  24.6 us
    concatenate x4, local copies, waits for them, and re-layouts, local(): jnp.concatenate([conv_terms.reshape(devices, -1), out_terms.reshape(devic...  24.3 us
    ppermute x4, starting transfers between devices, from_behind(): return lax.ppermute(block, axis, route)  12.4 us
    dot_general x3, matrix products, matmul(): jnp.dot(left, right, precision=lax.Precision.HIGHEST, preferred_element_t...  12 us
  transfers between devices with their start and end apart: 5, of which 4 were waited for; matrix products, arithmetic and copies ran while one was open for 4% of the time, Pallas kernels for 0%

profile of v1, /device:TPU:10, one launch (start us, length us, event | category | flops | bytes accessed | tf_op | source)
XLA Modules:
  0.0 535.9 jit_solution(6232266802496668457)
XLA Ops:
  7.2 0.0 copy-start.17
  7.2 0.0 reduce-scatter.2.cloned.1.call-start
  7.2 1.2 copy.36
  8.5 0.0 copy-start.3
  8.5 3.8 collective-permute-start
  12.4 0.0 copy-done.17
  12.4 1.3 slice_bitcast_fusion
  13.7 8.9 %collective-permute-done = f32[256,256]{0,1:T(8,128)S(1)} collective-permute-done((f32[256,256]{0,1:T(8,128)S(1)}, f32[256,256]{0,1:T(8,128)S(1)}, u32[]{:S(2)}, u32[]{:S(2)}) %collective-permute-start) | collective-permute-done | bytes 262176 | tf_op jit(solution)/shard_map/ppermute | solution.py:15
  22.6 5.3 fusion.12
  27.8 0.0 copy-done.3
  27.9 0.0 copy-done.13
  27.9 0.0 copy-start.8
  27.9 1.4 convolution_add_fusion
  29.3 0.0 copy-done.8
  29.3 2.1 collective-permute-start.1
  31.4 2.1 copy.34
  33.5 2.0 copy.35
  35.5 10.9 %collective-permute-done.1 = f32[512,256]{0,1:T(8,128)S(1)} collective-permute-done((f32[512,256]{0,1:T(8,128)S(1)}, f32[512,256]{0,1:T(8,128)S(1)}, u32[]{:S(2)}, u32[]{:S(2)}) %collective-permute-start.1) | collective-permute-done | bytes 524320 | tf_op jit(solution)/shard_map/ppermute | solution.py:15
  46.4 5.3 fusion.15
  51.7 0.0 copy-done.10
  51.7 0.0 copy-done.15
  51.7 0.0 copy-done.16
  51.8 0.0 copy-start
  51.8 2.3 subtract_multiply_fusion.3
  54.0 0.0 copy-done
  54.1 3.6 fusion
  57.7 2.2 collective-permute-start.2
  59.9 4.9 fusion.21
  64.8 2.1 fusion.30
  66.9 0.0 copy-start.9
  66.9 4.9 collective-permute-done.2
  71.8 0.2 fusion.38
  72.0 0.0 copy-start.11
  72.0 2.1 fusion.33
  74.1 3.3 subtract_multiply_fusion.1
  77.4 1.5 pad_maximum_fusion.3
  78.9 4.3 concatenate.52
  83.2 5.1 copy.45
  88.3 0.0 copy-done.1
  88.3 3.6 fusion.19
  91.9 2.5 pad_maximum_fusion
  94.4 6.6 %concatenate.50 = f32[4,2,8,2,2,4096]{5,4,3,2,1,0:T(2,128)} reshape(f32[1024,1024]{1,0:T(8,128)} %pad_maximum_fusion) | data formatting | bytes 8388608 | tf_op jit(solution)/shard_map/concatenate | solution.py:105
  101.0 8.3 %copy.44 = f32[4,2,8,2,2,4096]{5,1,3,0,2,4:T(2,128)} copy(f32[4,2,8,2,2,4096]{5,4,3,2,1,0:T(2,128)} %concatenate.50) | data formatting | bytes 8388608 | tf_op jit(solution)/shard_map/concatenate | solution.py:105
  109.3 10.7 %maximum_bitcast_fusion = f32[2,8,4,2,2,6144]{5,4,3,2,1,0:T(2,128)} fusion(f32[4,2,8,2,2,2048]{5,1,3,0,2,4:T(2,128)} %copy.45, f32[4,2,8,2,2,4096]{5,1,3,0,2,4:T(2,128)} %copy.44), kind=kLoop, calls=%fused_computation | loop fusion | flops 1572864 | bytes 12582912 | tf_op jit(solution)/shard_map/transpose | solution.py:110
  120.0 9.0 %reshape.31 = f32[2048,768]{1,0:T(8,128)} reshape(f32[2,8,4,2,2,6144]{5,4,3,2,1,0:T(2,128)} %maximum_bitcast_fusion) | data formatting | bytes 12582912 | tf_op jit(solution)/shard_map/reshape | solution.py:111
  129.0 0.0 reduce-scatter.2.cloned.1.call-update
  129.0 5.4 %fusion.4 = f32[512,512]{0,1:T(8,128)S(1)} fusion(f32[2,512,1024]{2,1,0:T(8,128)} %param.9, f32[512,512]{0,1:T(8,128)} %get-tuple-element.17, f32[512,512]{0,1:T(8,128)S(1)} %get-tuple-element.16), kind=kOutput, calls=%fused_computation.9 | convolution fusion | flops 3221749760 | bytes 5242880 | tf_op jit(solution)/shard_map/dot_general | solution.py:23
  134.5 0.0 copy-start.6
  134.5 1.0 copy-done.6
  135.5 0.7 fusion.55
  136.2 4.3 collective-permute-start.3
  140.5 0.2 fusion.20
  140.7 1.0 copy-done.2
  141.8 0.2 fusion.18
  142.0 74.2 %all-reduce = f32[2048]{0:T(1024)S(1)} all-reduce(f32[2048]{0:T(1024)S(1)} %maximum_multiply_fusion), channel_id=3, replica_groups=mesh['y'=4,'xl'=2,'z'=8,'xh'=2,'c'=2] {'y','xl','z','xh','c'}, use_global_device_ids=true, to_apply=%region_3.0.clone | all-reduce | flops 2048 | bytes 16384
  216.2 0.6 dynamic-slice
  216.8 0.0 collective-permute-done.3
  216.8 0.0 copy-done.12
  216.8 1.1 fusion.37
  217.9 1.0 copy.46
  218.9 308.0 %reduce-scatter.2.cloned.1.call-done = f32[8,768]{1,0:T(8,128)} async-done(((f32[2048,768]{1,0:T(8,128)}), f32[8,768]{1,0:T(8,128)}) %reduce-scatter.2.cloned.1.call-update) | async-done | bytes 24592 | tf_op jit(solution)/shard_map/reduce_scatter | solution.py:112
  526.9 0.7 broadcast_multiply_fusion
  527.7 0.6 slice.109
  528.3 0.6 slice.108
  (23 shorter events, 0.1 us)
Async XLA Ops:
  7.2 5.2 copy-start.17
  7.2 519.7 %reduce-scatter.2.cloned.1.call-start = ((), (), s32[]{:S(2)}) async-start(), calls=%async_computation.1 | async-start | bytes 6316032 | tf_op jit(solution)/shard_map/reduce_scatter | solution.py:112
  8.5 19.4 %copy-start.3 = (f32[1,512,256]{1,2,0:T(8,128)}, f32[1,512,256]{1,2,0:T(8,128)S(1)}, u32[]{:S(2)}) copy-start(f32[1,512,256]{1,2,0:T(8,128)S(1)} %copy.36) | copy-start | bytes 1572868
  8.5 14.0 %collective-permute-start = (f32[256,256]{0,1:T(8,128)S(1)}, f32[256,256]{0,1:T(8,128)S(1)}, u32[]{:S(2)}, u32[]{:S(2)}) collective-permute-start(f32[256,256]{0,1:T(8,128)S(1)} %get-tuple-element.22), channel_id=1, source_target_pairs={{0,4},{4,8},{8,12},{12,16},{16,20},{20,24},{24,28},{28,32},{32,36}... | collective-permute-start | bytes 786440 | tf_op jit(solution)/shard_map/ppermute | solution.py:15
  22.6 5.3 copy-start.13
  27.9 1.4 copy-start.8
  29.3 17.1 %collective-permute-start.1 = (f32[512,256]{0,1:T(8,128)S(1)}, f32[512,256]{0,1:T(8,128)S(1)}, u32[]{:S(2)}, u32[]{:S(2)}) collective-permute-start(f32[512,256]{0,1:T(8,128)S(1)} %convolution_add_fusion), channel_id=1, source_target_pairs={{0,4},{4,8},{8,12},{12,16},{16,20},{20,24},{24,28},{28,32},{32,36}... | collective-permute-start | bytes 1572872 | tf_op jit(solution)/shard_map/ppermute | solution.py:15
  46.4 5.3 copy-start.10
  46.4 5.4 copy-start.15
  46.4 5.4 %copy-start.16 = (f32[1,512,256]{1,2,0:T(8,128)S(1)}, f32[1,512,256]{1,2,0:T(8,128)}, u32[]{:S(2)}) copy-start(f32[1,512,256]{1,2,0:T(8,128)} %copy.35) | copy-start | bytes 1572868
  51.8 2.3 copy-start
  57.7 14.1 %collective-permute-start.2 = (f32[512,256]{0,1:T(8,128)S(1)}, f32[512,256]{0,1:T(8,128)S(1)}, u32[]{:S(2)}, u32[]{:S(2)}) collective-permute-start(f32[512,256]{0,1:T(8,128)S(1)} %slice.104), channel_id=1, source_target_pairs={{4,0},{8,4},{12,8},{16,12},{20,16},{24,20},{28,24},{32,28},{36,32}... | collective-permute-start | bytes 1572872 | tf_op jit(solution)/shard_map/ppermute | solution.py:15
  66.9 5.1 copy-start.9
  72.0 2.1 copy-start.11
  83.2 5.1 copy-start.1
  83.2 5.1 copy-start.4
  83.2 5.1 copy-start.14
  88.3 3.6 copy-start.5
  134.5 1.0 copy-start.6
  136.2 80.6 %collective-permute-start.3 = (f32[256,256]{0,1:T(8,128)}, f32[256,256]{0,1:T(8,128)}, u32[]{:S(2)}, u32[]{:S(2)}) collective-permute-start(f32[256,256]{0,1:T(8,128)} %get-tuple-element.21), channel_id=1, source_target_pairs={{4,0},{8,4},{12,8},{16,12},{20,16},{24,20},{28,24},{32,28},{36,32}... | collective-permute-start | bytes 786440 | tf_op jit(solution)/shard_map/ppermute | solution.py:15
  140.5 1.2 copy-start.2
  141.8 75.0 %copy-start.7 = (f32[512,512]{0,1:T(8,128)S(1)}, f32[512,512]{0,1:T(8,128)}, u32[]{:S(2)}) copy-start(f32[512,512]{0,1:T(8,128)} %copy-done.6) | copy-start | bytes 3145732
  141.8 75.0 %copy-start.12 = (f32[512,256]{0,1:T(8,128)S(1)}, f32[512,256]{0,1:T(8,128)}, u32[]{:S(2)}) copy-start(f32[512,256]{0,1:T(8,128)} %copy-done.11) | copy-start | bytes 1572868
Sparse Core Ops, SparseCore 0:
  129.2 397.7 reduce-scatter.1
